TPU v7x, 256 devices: a whole 4x4x8 slice. The times are simulated.
256 devices in a mesh: sec: 16 (over x, y), vel: 16 (over z, core).
Axes of the slice: x: 4, y: 4, z: 8, core: 2. Of those that a mesh axis runs over, the one named last changes fastest.
Arguments:
- distribution: float32 [13824, 4096], P('vel', 'sec'), may hold values from -6 to 6
- collision: float32 [4096], P('sec'), may hold values from 0.05 to 2
- lower_blocks: float32 [25, 4096], P(None, 'sec'), may hold values from -0.6 to 0.6
- upper_blocks: float32 [25, 4096], P(None, 'sec'), may hold values from -0.6 to 0.6
- diag_inverse: float32 [25, 4096], P(None, 'sec'), may hold values from -0.2 to 1.4
Outputs:
- new_distribution: float32 [13824, 4096], P('vel', 'sec')
- macro: float32 [5, 4096], P(None, 'sec')
All inputs are finite; a program needn't handle non-finite values.
Results may differ from a plain program's by a relative error of at most 0.0003.
Values sent between devices are 32-bit elements; how exact they have to be, the bound alone decides.
No kernel may reach another device: no remote copies, remote signals or barrier semaphores. Data moves between devices by JAX's collectives and lax.ppermute only.
A program may use at most 64 MiB of HBM per device.

v0:
```python
import math
import jax
import jax.numpy as jnp
import numpy as np
from jax import lax
from jax.sharding import PartitionSpec as P

NXI = 24
TUBES = 128
JACOBI = 4
NEWTON = 2
HIGH = lax.Precision.HIGHEST
pseudo_rate = 1.0


def passed_along(block, axis, distance):
    devices = range(lax.axis_size(axis))
    route = [(i - distance, i) for i in devices if i - distance in devices]
    return lax.ppermute(block, axis, route)


def extended(array, sides, width):
    for axis, dim in sides:
        count, length = (lax.axis_size(axis), array.shape[dim])
        up = [(i, (i + 1) % count) for i in range(count - 1)]
        down = [(j, i) for i, j in up]
        last = lax.slice_in_dim(array, length - width, length, axis=dim)
        first = lax.slice_in_dim(array, 0, width, axis=dim)
        before = lax.ppermute(last, axis, up)
        after = lax.ppermute(first, axis, down)
        array = jnp.concatenate([before, array, after], axis=dim)
    return array


def hermite_rule(count):
    quarter = math.pi ** (-0.25)
    found = []
    last_slope = 1.0
    for index in range(count // 2):
        if index == 0:
            guess = math.sqrt(2.0 * count + 1.0) - 1.85575 * (2.0 * count + 1.0) ** (-0.16667)
        elif index == 1:
            guess = guess - 1.14 * count**0.426 / guess
        elif index == 2:
            guess = 1.86 * guess - 0.86 * found[0][0]
        elif index == 3:
            guess = 1.91 * guess - 0.91 * found[1][0]
        else:
            guess = 2.0 * guess - found[index - 2][0]
        for repeat in range(60):
            current = quarter
            previous = 0.0
            for order in range(count):
                older = previous
                previous = current
                current = (
                    guess * math.sqrt(2.0 / (order + 1)) * previous
                    - math.sqrt(order / (order + 1.0)) * older
                )
            last_slope = math.sqrt(2.0 * count) * previous
            guess = guess - current / last_slope
        found.append((guess, 2.0 / (last_slope * last_slope)))
    positive = found[::-1]
    points = [-pair[0] for pair in found] + [pair[0] for pair in positive]
    weights = [pair[1] for pair in found] + [pair[1] for pair in positive]
    return (np.array(points), np.array(weights))


def node_tables(axis_points):
    points, weights = hermite_rule(axis_points)
    node_index = np.arange(axis_points**3)
    idx_x = node_index % axis_points
    idx_z = node_index // axis_points % axis_points
    idx_y = node_index // (axis_points * axis_points)
    along_x = points[idx_x]
    along_y = points[idx_y]
    along_z = points[idx_z]
    node_weight = weights[idx_x] * weights[idx_y] * weights[idx_z] / math.pi**1.5
    energy = along_x**2 + along_y**2 + along_z**2 - 1.5
    moment_basis = np.stack([along_x * 0.0 + 1.0, along_x, along_y, along_z, energy])
    norm_scale = np.array([1.0, 0.5, 0.5, 0.5, 1.5])
    return (
        along_x,
        node_weight,
        moment_basis * node_weight[None, :],
        moment_basis / norm_scale[:, None],
    )


def apply_block(matrices, vector):
    shaped = matrices.reshape((5, 5) + vector.shape[1:])
    return jnp.sum(shaped * vector[None], axis=1)


def affine_combine(earlier_map, later_map):
    return (later_map[0] * earlier_map[0], later_map[0] * earlier_map[1] + later_map[1])


def newton_sums(loaded, signed, shift_mass, shift_flow):
    growth = jnp.exp(shift_mass + shift_flow * signed)
    scaled = loaded * growth
    excess = loaded * (growth - 1.0)
    return jnp.stack(
        [
            jnp.sum(scaled),
            jnp.sum(scaled * signed),
            jnp.sum(scaled * signed * signed),
            jnp.sum(excess),
            jnp.sum(excess * signed),
        ]
    )


def newton_update(shift_mass, shift_flow, sums, goal_mass, goal_flow):
    resid_mass = sums[3] - goal_mass
    resid_flow = sums[4] - goal_flow
    determinant = sums[0] * sums[2] - sums[1] * sums[1]
    new_mass = shift_mass - (sums[2] * resid_mass - sums[1] * resid_flow) / determinant
    new_flow = shift_flow - (sums[0] * resid_flow - sums[1] * resid_mass) / determinant
    return (new_mass, new_flow)


def body(distribution, collision, lower_blocks, upper_blocks, diag_inverse):
    node_count = distribution.shape[0]
    cell_count = distribution.shape[1]
    length = cell_count // TUBES
    node_rows = node_count // NXI
    half_nodes = NXI // 2
    along_x, node_weight, weighted_np, rebuild_np = node_tables(NXI)
    all_signed = jnp.asarray(along_x, jnp.float32)
    all_mass = jnp.asarray(node_weight, jnp.float32)
    offset = lax.axis_index("vel") * node_count
    weighted = lax.dynamic_slice_in_dim(
        jnp.asarray(weighted_np, jnp.float32), offset, node_count, 1
    )
    rebuild = lax.dynamic_slice_in_dim(jnp.asarray(rebuild_np, jnp.float32), offset, node_count, 1)
    signed = lax.dynamic_slice_in_dim(all_signed, offset, node_count, 0)
    node_mass = lax.dynamic_slice_in_dim(all_mass, offset, node_count, 0)
    old_moments = lax.psum(jnp.dot(weighted, distribution, precision=HIGH), "vel")
    target = jnp.dot(rebuild.T, old_moments, precision=HIGH)
    total_length = length * lax.axis_size("sec")
    thickness = collision.reshape(1, 1, length, TUBES)
    node_speed = jnp.abs(signed).reshape(node_rows, NXI, 1, 1)
    denominator = node_speed * total_length + thickness + pseudo_rate
    carry_rate = node_speed * total_length / denominator
    drive_term = (
        thickness * target.reshape(node_rows, NXI, length, TUBES)
        + pseudo_rate * distribution.reshape(node_rows, NXI, length, TUBES)
    ) / denominator
    prod_neg, local_neg = lax.associative_scan(
        affine_combine,
        (carry_rate[:, :half_nodes], drive_term[:, :half_nodes]),
        reverse=True,
        axis=2,
    )
    prod_pos, local_pos = lax.associative_scan(
        affine_combine, (carry_rate[:, half_nodes:], drive_term[:, half_nodes:]), axis=2
    )
    summary_pos = (prod_pos[:, :, -1], local_pos[:, :, -1])
    summary_neg = (prod_neg[:, :, 0], local_neg[:, :, 0])

    def relay(turn_index, inflows):
        out_pos = summary_pos[0] * inflows[0] + summary_pos[1]
        out_neg = summary_neg[0] * inflows[1] + summary_neg[1]
        return (passed_along(out_pos, "sec", 1), passed_along(out_neg, "sec", -1))

    start_flows = (jnp.zeros_like(summary_pos[1]), jnp.zeros_like(summary_neg[1]))
    inflow_pos, inflow_neg = lax.fori_loop(0, lax.axis_size("sec") - 1, relay, start_flows)
    field_neg = local_neg + prod_neg * inflow_neg[:, :, None, :]
    field_pos = local_pos + prod_pos * inflow_pos[:, :, None, :]
    half_field = jnp.concatenate([field_neg, field_pos], axis=1).reshape(node_count, cell_count)
    half_moments = lax.psum(jnp.dot(weighted, half_field, precision=HIGH), "vel")
    residual = (half_moments - old_moments).reshape(5, length, TUBES)
    lower_r = lower_blocks.reshape(25, length, TUBES)
    upper_r = upper_blocks.reshape(25, length, TUBES)
    inverse_r = diag_inverse.reshape(25, length, TUBES)
    correction = apply_block(inverse_r, residual)
    for sweep_index in range(JACOBI):
        padded = extended(correction, (("sec", 1),), 1)
        correction = apply_block(
            inverse_r,
            residual - apply_block(lower_r, padded[:, :-2]) - apply_block(upper_r, padded[:, 2:]),
        )
    correction = correction.reshape(5, cell_count)
    macro = half_moments + correction
    synthetic = half_field + jnp.dot(rebuild.T, correction, precision=HIGH)
    local_totals = jnp.sum(old_moments - macro, axis=1)[0:2]
    magnitude = jnp.sum(jnp.abs(synthetic), axis=1)
    shift_mass = jnp.zeros((), jnp.float32)
    shift_flow = jnp.zeros((), jnp.float32)
    goals = lax.psum(local_totals, "sec")
    loaded = node_mass * magnitude
    for newton_turn in range(NEWTON):
        sums = lax.psum(newton_sums(loaded, signed, shift_mass, shift_flow), ("sec", "vel"))
        shift_mass, shift_flow = newton_update(shift_mass, shift_flow, sums, goals[0], goals[1])
    growth = jnp.exp(shift_mass + shift_flow * signed)
    new_distribution = synthetic + jnp.abs(synthetic) * (growth[:, None] - 1.0)
    return (new_distribution, macro)


def solution(mesh):
    in_specs = (P("vel", "sec"), P("sec"), P(None, "sec"), P(None, "sec"), P(None, "sec"))
    out_specs = (P("vel", "sec"), P(None, "sec"))
    return jax.shard_map(body, mesh=mesh, in_specs=in_specs, out_specs=out_specs, check_vma=False)
```

profile of v0, /device:TPU:1, one launch (start us, length us, event | category | flops | bytes accessed | tf_op | source)
XLA Modules:
  0.0 529.8 jit_solution(13319355678150819827)
XLA Ops:
  3.6 27.9 %psum.35 = f32[5,256]{1,0:T(8,128)S(1)} all-reduce(f32[5,256]{1,0:T(8,128)S(1)} %fusion.12), channel_id=1, replica_groups=mesh['sec'=16,'vel'=16] {'vel'}, use_global_device_ids=true, to_apply=%region_0.0 | all-reduce | flops 1280 | bytes 10240 | tf_op jit(solution)/shard_map/psum | solution.py:139
  39.4 2.0 rev.8
  41.5 2.0 rev.9
  44.4 185.1 %while.12 = (s32[]{:T(128)}, f32[36,12,128]{2,1,0:T(8,128)S(1)}, f32[36,12,128]{2,1,0:T(8,128)S(1)}, f32[36,12,128]{2,1,0:T(8,128)S(1)}, f32[36,12,128]{2,1,0:T(...) while((s32[]{:T(128)}, f32[36,12,128]{2,1,0:T(8,128)S(1)}, ...), condition=%wide.region_2.0_spmd, body=%wide.region_1.0_spmd.sunk | while | flops 221186 | bytes 3539109 | solution.py:168
  44.5 3.2 collective-permute-start
  49.1 2.3 collective-permute-done
  51.3 3.9 collective-permute-done.1
  55.3 3.5 collective-permute-start
  60.2 2.3 collective-permute-done
  62.4 3.9 collective-permute-done.1
  66.4 4.4 collective-permute-start
  72.2 2.3 collective-permute-done
  74.5 3.9 collective-permute-done.1
  78.4 4.0 collective-permute-start
  83.9 2.3 collective-permute-done
  86.1 3.9 collective-permute-done.1
  90.1 4.0 collective-permute-start
  95.5 2.3 collective-permute-done
  97.7 3.9 collective-permute-done.1
  101.7 3.7 collective-permute-start
  106.8 2.3 collective-permute-done
  109.1 4.0 collective-permute-done.1
  113.1 3.9 collective-permute-start
  118.5 3.2 collective-permute-done
  121.7 4.2 collective-permute-done.1
  125.9 3.7 collective-permute-start
  131.0 4.3 collective-permute-done
  135.3 4.4 collective-permute-done.1
  139.8 3.7 collective-permute-start
  144.9 5.2 collective-permute-done
  150.1 4.2 collective-permute-done.1
  154.3 3.8 collective-permute-start
  159.6 4.3 collective-permute-done
  163.9 3.9 collective-permute-done.1
  167.8 4.8 collective-permute-start
  174.0 3.7 collective-permute-done
  177.7 3.9 collective-permute-done.1
  181.7 4.3 collective-permute-start
  187.3 2.7 collective-permute-done
  190.1 3.9 collective-permute-done.1
  194.1 4.3 collective-permute-start
  199.7 2.3 collective-permute-done
  202.0 3.9 collective-permute-done.1
  206.0 4.0 collective-permute-start
  211.4 2.3 collective-permute-done
  213.6 3.9 collective-permute-done.1
  217.6 4.3 collective-permute-start
  223.3 2.3 collective-permute-done
  225.6 3.9 collective-permute-done.1
  232.6 44.9 %psum.36 = f32[5,256]{1,0:T(8,128)S(1)} all-reduce(f32[5,256]{1,0:T(8,128)S(1)} %fusion), channel_id=1, replica_groups=mesh['sec'=16,'vel'=16] {'vel'}, use_global_device_ids=true, to_apply=%region_3.0 | all-reduce | flops 1280 | bytes 10240 | tf_op jit(solution)/shard_map/psum | solution.py:172
  277.7 3.7 collective-permute-start.2
  282.8 3.2 collective-permute-done.3
  286.1 3.7 collective-permute-start.4
  291.2 3.0 collective-permute-done.5
  294.3 4.0 collective-permute-start.6
  299.7 3.0 collective-permute-done.7
  302.8 4.0 collective-permute-start.8
  308.2 3.0 collective-permute-done.9
  312.0 1.9 abs_reduce_fusion
  314.0 30.6 %psum.38 = f32[2]{0:T(128)S(1)} all-reduce(f32[2]{0:T(128)S(1)} %bitcast.57), channel_id=1, replica_groups=mesh['sec'=16,'vel'=16] {'sec'}, use_global_device_ids=true, to_apply=%region_25.0 | all-reduce | flops 2 | bytes 16 | tf_op jit(solution)/shard_map/psum | solution.py:191
  346.1 3.2 stack.41
  349.9 82.5 %psum.37 = f32[5]{0:T(128)S(1)} all-reduce(f32[5]{0:T(128)S(1)} %stack.41), channel_id=1, replica_groups=mesh['sec'=16,'vel'=16] {'sec','vel'}, use_global_device_ids=true, to_apply=%region_23.0 | all-reduce | flops 5 | bytes 40 | tf_op jit(solution)/shard_map/psum | solution.py:194
  442.2 3.2 stack.47
  445.4 74.4 %psum.39 = f32[5]{0:T(128)S(1)} all-reduce(f32[5]{0:T(128)S(1)} %stack.47), channel_id=1, replica_groups=mesh['sec'=16,'vel'=16] {'sec','vel'}, use_global_device_ids=true, to_apply=%region_31.0 | all-reduce | flops 5 | bytes 40 | tf_op jit(solution)/shard_map/psum | solution.py:194
  (126 shorter events, 49.0 us)
Async XLA Ops:
  0.6 1.7 copy-start
  34.7 0.7 copy-start.6
  44.5 6.9 %collective-permute-start = (f32[36,12,128]{2,1,0:T(8,128)S(1)}, f32[36,12,128]{2,1,0:T(8,128)S(1)}, u32[]{:S(2)}, u32[]{:S(2)}) collective-permute-start(f32[36,12,128]{2,1,0:T(8,128)S(1)} %multiply_add_fusion.6), channel_id=1, source_target_pairs={{0,16},{16,32},{32,48},{48,64},{64,80},{80,96},{96,112},{112,128},... | collective-permute-start | bytes 663560 | tf_op jit(solution)/shard_map/while/body/eval_jaxpr/ppermute | solution.py:19
  47.8 7.5 %collective-permute-start.1 = (f32[36,12,128]{2,1,0:T(8,128)S(1)}, f32[36,12,128]{2,1,0:T(8,128)S(1)}, u32[]{:S(2)}, u32[]{:S(2)}) collective-permute-start(f32[36,12,128]{2,1,0:T(8,128)S(1)} %multiply_add_fusion.7), channel_id=1, source_target_pairs={{16,0},{32,16},{48,32},{64,48},{80,64},{96,80},{112,96},{128,112},... | collective-permute-start | bytes 663560 | tf_op jit(solution)/shard_map/while/body/eval_jaxpr/ppermute | solution.py:19
  55.3 7.1 %collective-permute-start = (f32[36,12,128]{2,1,0:T(8,128)S(1)}, f32[36,12,128]{2,1,0:T(8,128)S(1)}, u32[]{:S(2)}, u32[]{:S(2)}) collective-permute-start(f32[36,12,128]{2,1,0:T(8,128)S(1)} %multiply_add_fusion.6), channel_id=1, source_target_pairs={{0,16},{16,32},{32,48},{48,64},{64,80},{80,96},{96,112},{112,128},... | collective-permute-start | bytes 663560 | tf_op jit(solution)/shard_map/while/body/eval_jaxpr/ppermute | solution.py:19
  58.9 7.5 %collective-permute-start.1 = (f32[36,12,128]{2,1,0:T(8,128)S(1)}, f32[36,12,128]{2,1,0:T(8,128)S(1)}, u32[]{:S(2)}, u32[]{:S(2)}) collective-permute-start(f32[36,12,128]{2,1,0:T(8,128)S(1)} %multiply_add_fusion.7), channel_id=1, source_target_pairs={{16,0},{32,16},{48,32},{64,48},{80,64},{96,80},{112,96},{128,112},... | collective-permute-start | bytes 663560 | tf_op jit(solution)/shard_map/while/body/eval_jaxpr/ppermute | solution.py:19
  66.4 8.1 %collective-permute-start = (f32[36,12,128]{2,1,0:T(8,128)S(1)}, f32[36,12,128]{2,1,0:T(8,128)S(1)}, u32[]{:S(2)}, u32[]{:S(2)}) collective-permute-start(f32[36,12,128]{2,1,0:T(8,128)S(1)} %multiply_add_fusion.6), channel_id=1, source_target_pairs={{0,16},{16,32},{32,48},{48,64},{64,80},{80,96},{96,112},{112,128},... | collective-permute-start | bytes 663560 | tf_op jit(solution)/shard_map/while/body/eval_jaxpr/ppermute | solution.py:19
  70.9 7.5 %collective-permute-start.1 = (f32[36,12,128]{2,1,0:T(8,128)S(1)}, f32[36,12,128]{2,1,0:T(8,128)S(1)}, u32[]{:S(2)}, u32[]{:S(2)}) collective-permute-start(f32[36,12,128]{2,1,0:T(8,128)S(1)} %multiply_add_fusion.7), channel_id=1, source_target_pairs={{16,0},{32,16},{48,32},{64,48},{80,64},{96,80},{112,96},{128,112},... | collective-permute-start | bytes 663560 | tf_op jit(solution)/shard_map/while/body/eval_jaxpr/ppermute | solution.py:19
  78.4 7.7 %collective-permute-start = (f32[36,12,128]{2,1,0:T(8,128)S(1)}, f32[36,12,128]{2,1,0:T(8,128)S(1)}, u32[]{:S(2)}, u32[]{:S(2)}) collective-permute-start(f32[36,12,128]{2,1,0:T(8,128)S(1)} %multiply_add_fusion.6), channel_id=1, source_target_pairs={{0,16},{16,32},{32,48},{48,64},{64,80},{80,96},{96,112},{112,128},... | collective-permute-start | bytes 663560 | tf_op jit(solution)/shard_map/while/body/eval_jaxpr/ppermute | solution.py:19
  82.5 7.5 %collective-permute-start.1 = (f32[36,12,128]{2,1,0:T(8,128)S(1)}, f32[36,12,128]{2,1,0:T(8,128)S(1)}, u32[]{:S(2)}, u32[]{:S(2)}) collective-permute-start(f32[36,12,128]{2,1,0:T(8,128)S(1)} %multiply_add_fusion.7), channel_id=1, source_target_pairs={{16,0},{32,16},{48,32},{64,48},{80,64},{96,80},{112,96},{128,112},... | collective-permute-start | bytes 663560 | tf_op jit(solution)/shard_map/while/body/eval_jaxpr/ppermute | solution.py:19
  90.1 7.7 %collective-permute-start = (f32[36,12,128]{2,1,0:T(8,128)S(1)}, f32[36,12,128]{2,1,0:T(8,128)S(1)}, u32[]{:S(2)}, u32[]{:S(2)}) collective-permute-start(f32[36,12,128]{2,1,0:T(8,128)S(1)} %multiply_add_fusion.6), channel_id=1, source_target_pairs={{0,16},{16,32},{32,48},{48,64},{64,80},{80,96},{96,112},{112,128},... | collective-permute-start | bytes 663560 | tf_op jit(solution)/shard_map/while/body/eval_jaxpr/ppermute | solution.py:19
  94.2 7.5 %collective-permute-start.1 = (f32[36,12,128]{2,1,0:T(8,128)S(1)}, f32[36,12,128]{2,1,0:T(8,128)S(1)}, u32[]{:S(2)}, u32[]{:S(2)}) collective-permute-start(f32[36,12,128]{2,1,0:T(8,128)S(1)} %multiply_add_fusion.7), channel_id=1, source_target_pairs={{16,0},{32,16},{48,32},{64,48},{80,64},{96,80},{112,96},{128,112},... | collective-permute-start | bytes 663560 | tf_op jit(solution)/shard_map/while/body/eval_jaxpr/ppermute | solution.py:19
  101.7 7.4 %collective-permute-start = (f32[36,12,128]{2,1,0:T(8,128)S(1)}, f32[36,12,128]{2,1,0:T(8,128)S(1)}, u32[]{:S(2)}, u32[]{:S(2)}) collective-permute-start(f32[36,12,128]{2,1,0:T(8,128)S(1)} %multiply_add_fusion.6), channel_id=1, source_target_pairs={{0,16},{16,32},{32,48},{48,64},{64,80},{80,96},{96,112},{112,128},... | collective-permute-start | bytes 663560 | tf_op jit(solution)/shard_map/while/body/eval_jaxpr/ppermute | solution.py:19
  105.5 7.6 %collective-permute-start.1 = (f32[36,12,128]{2,1,0:T(8,128)S(1)}, f32[36,12,128]{2,1,0:T(8,128)S(1)}, u32[]{:S(2)}, u32[]{:S(2)}) collective-permute-start(f32[36,12,128]{2,1,0:T(8,128)S(1)} %multiply_add_fusion.7), channel_id=1, source_target_pairs={{16,0},{32,16},{48,32},{64,48},{80,64},{96,80},{112,96},{128,112},... | collective-permute-start | bytes 663560 | tf_op jit(solution)/shard_map/while/body/eval_jaxpr/ppermute | solution.py:19
  113.1 8.5 %collective-permute-start = (f32[36,12,128]{2,1,0:T(8,128)S(1)}, f32[36,12,128]{2,1,0:T(8,128)S(1)}, u32[]{:S(2)}, u32[]{:S(2)}) collective-permute-start(f32[36,12,128]{2,1,0:T(8,128)S(1)} %multiply_add_fusion.6), channel_id=1, source_target_pairs={{0,16},{16,32},{32,48},{48,64},{64,80},{80,96},{96,112},{112,128},... | collective-permute-start | bytes 663560 | tf_op jit(solution)/shard_map/while/body/eval_jaxpr/ppermute | solution.py:19
  117.2 8.7 %collective-permute-start.1 = (f32[36,12,128]{2,1,0:T(8,128)S(1)}, f32[36,12,128]{2,1,0:T(8,128)S(1)}, u32[]{:S(2)}, u32[]{:S(2)}) collective-permute-start(f32[36,12,128]{2,1,0:T(8,128)S(1)} %multiply_add_fusion.7), channel_id=1, source_target_pairs={{16,0},{32,16},{48,32},{64,48},{80,64},{96,80},{112,96},{128,112},... | collective-permute-start | bytes 663560 | tf_op jit(solution)/shard_map/while/body/eval_jaxpr/ppermute | solution.py:19
  125.9 9.4 %collective-permute-start = (f32[36,12,128]{2,1,0:T(8,128)S(1)}, f32[36,12,128]{2,1,0:T(8,128)S(1)}, u32[]{:S(2)}, u32[]{:S(2)}) collective-permute-start(f32[36,12,128]{2,1,0:T(8,128)S(1)} %multiply_add_fusion.6), channel_id=1, source_target_pairs={{0,16},{16,32},{32,48},{48,64},{64,80},{80,96},{96,112},{112,128},... | collective-permute-start | bytes 663560 | tf_op jit(solution)/shard_map/while/body/eval_jaxpr/ppermute | solution.py:19
  129.7 10.1 %collective-permute-start.1 = (f32[36,12,128]{2,1,0:T(8,128)S(1)}, f32[36,12,128]{2,1,0:T(8,128)S(1)}, u32[]{:S(2)}, u32[]{:S(2)}) collective-permute-start(f32[36,12,128]{2,1,0:T(8,128)S(1)} %multiply_add_fusion.7), channel_id=1, source_target_pairs={{16,0},{32,16},{48,32},{64,48},{80,64},{96,80},{112,96},{128,112},... | collective-permute-start | bytes 663560 | tf_op jit(solution)/shard_map/while/body/eval_jaxpr/ppermute | solution.py:19
  139.8 10.2 %collective-permute-start = (f32[36,12,128]{2,1,0:T(8,128)S(1)}, f32[36,12,128]{2,1,0:T(8,128)S(1)}, u32[]{:S(2)}, u32[]{:S(2)}) collective-permute-start(f32[36,12,128]{2,1,0:T(8,128)S(1)} %multiply_add_fusion.6), channel_id=1, source_target_pairs={{0,16},{16,32},{32,48},{48,64},{64,80},{80,96},{96,112},{112,128},... | collective-permute-start | bytes 663560 | tf_op jit(solution)/shard_map/while/body/eval_jaxpr/ppermute | solution.py:19
  143.6 10.7 %collective-permute-start.1 = (f32[36,12,128]{2,1,0:T(8,128)S(1)}, f32[36,12,128]{2,1,0:T(8,128)S(1)}, u32[]{:S(2)}, u32[]{:S(2)}) collective-permute-start(f32[36,12,128]{2,1,0:T(8,128)S(1)} %multiply_add_fusion.7), channel_id=1, source_target_pairs={{16,0},{32,16},{48,32},{64,48},{80,64},{96,80},{112,96},{128,112},... | collective-permute-start | bytes 663560 | tf_op jit(solution)/shard_map/while/body/eval_jaxpr/ppermute | solution.py:19
  154.3 9.5 %collective-permute-start = (f32[36,12,128]{2,1,0:T(8,128)S(1)}, f32[36,12,128]{2,1,0:T(8,128)S(1)}, u32[]{:S(2)}, u32[]{:S(2)}) collective-permute-start(f32[36,12,128]{2,1,0:T(8,128)S(1)} %multiply_add_fusion.6), channel_id=1, source_target_pairs={{0,16},{16,32},{32,48},{48,64},{64,80},{80,96},{96,112},{112,128},... | collective-permute-start | bytes 663560 | tf_op jit(solution)/shard_map/while/body/eval_jaxpr/ppermute | solution.py:19
  158.3 9.5 %collective-permute-start.1 = (f32[36,12,128]{2,1,0:T(8,128)S(1)}, f32[36,12,128]{2,1,0:T(8,128)S(1)}, u32[]{:S(2)}, u32[]{:S(2)}) collective-permute-start(f32[36,12,128]{2,1,0:T(8,128)S(1)} %multiply_add_fusion.7), channel_id=1, source_target_pairs={{16,0},{32,16},{48,32},{64,48},{80,64},{96,80},{112,96},{128,112},... | collective-permute-start | bytes 663560 | tf_op jit(solution)/shard_map/while/body/eval_jaxpr/ppermute | solution.py:19
  167.8 9.9 %collective-permute-start = (f32[36,12,128]{2,1,0:T(8,128)S(1)}, f32[36,12,128]{2,1,0:T(8,128)S(1)}, u32[]{:S(2)}, u32[]{:S(2)}) collective-permute-start(f32[36,12,128]{2,1,0:T(8,128)S(1)} %multiply_add_fusion.6), channel_id=1, source_target_pairs={{0,16},{16,32},{32,48},{48,64},{64,80},{80,96},{96,112},{112,128},... | collective-permute-start | bytes 663560 | tf_op jit(solution)/shard_map/while/body/eval_jaxpr/ppermute | solution.py:19
  172.7 8.9 %collective-permute-start.1 = (f32[36,12,128]{2,1,0:T(8,128)S(1)}, f32[36,12,128]{2,1,0:T(8,128)S(1)}, u32[]{:S(2)}, u32[]{:S(2)}) collective-permute-start(f32[36,12,128]{2,1,0:T(8,128)S(1)} %multiply_add_fusion.7), channel_id=1, source_target_pairs={{16,0},{32,16},{48,32},{64,48},{80,64},{96,80},{112,96},{128,112},... | collective-permute-start | bytes 663560 | tf_op jit(solution)/shard_map/while/body/eval_jaxpr/ppermute | solution.py:19
  181.7 8.4 %collective-permute-start = (f32[36,12,128]{2,1,0:T(8,128)S(1)}, f32[36,12,128]{2,1,0:T(8,128)S(1)}, u32[]{:S(2)}, u32[]{:S(2)}) collective-permute-start(f32[36,12,128]{2,1,0:T(8,128)S(1)} %multiply_add_fusion.6), channel_id=1, source_target_pairs={{0,16},{16,32},{32,48},{48,64},{64,80},{80,96},{96,112},{112,128},... | collective-permute-start | bytes 663560 | tf_op jit(solution)/shard_map/while/body/eval_jaxpr/ppermute | solution.py:19
  186.0 8.0 %collective-permute-start.1 = (f32[36,12,128]{2,1,0:T(8,128)S(1)}, f32[36,12,128]{2,1,0:T(8,128)S(1)}, u32[]{:S(2)}, u32[]{:S(2)}) collective-permute-start(f32[36,12,128]{2,1,0:T(8,128)S(1)} %multiply_add_fusion.7), channel_id=1, source_target_pairs={{16,0},{32,16},{48,32},{64,48},{80,64},{96,80},{112,96},{128,112},... | collective-permute-start | bytes 663560 | tf_op jit(solution)/shard_map/while/body/eval_jaxpr/ppermute | solution.py:19
  194.1 8.0 %collective-permute-start = (f32[36,12,128]{2,1,0:T(8,128)S(1)}, f32[36,12,128]{2,1,0:T(8,128)S(1)}, u32[]{:S(2)}, u32[]{:S(2)}) collective-permute-start(f32[36,12,128]{2,1,0:T(8,128)S(1)} %multiply_add_fusion.6), channel_id=1, source_target_pairs={{0,16},{16,32},{32,48},{48,64},{64,80},{80,96},{96,112},{112,128},... | collective-permute-start | bytes 663560 | tf_op jit(solution)/shard_map/while/body/eval_jaxpr/ppermute | solution.py:19
  198.4 7.5 %collective-permute-start.1 = (f32[36,12,128]{2,1,0:T(8,128)S(1)}, f32[36,12,128]{2,1,0:T(8,128)S(1)}, u32[]{:S(2)}, u32[]{:S(2)}) collective-permute-start(f32[36,12,128]{2,1,0:T(8,128)S(1)} %multiply_add_fusion.7), channel_id=1, source_target_pairs={{16,0},{32,16},{48,32},{64,48},{80,64},{96,80},{112,96},{128,112},... | collective-permute-start | bytes 663560 | tf_op jit(solution)/shard_map/while/body/eval_jaxpr/ppermute | solution.py:19
  206.0 7.7 %collective-permute-start = (f32[36,12,128]{2,1,0:T(8,128)S(1)}, f32[36,12,128]{2,1,0:T(8,128)S(1)}, u32[]{:S(2)}, u32[]{:S(2)}) collective-permute-start(f32[36,12,128]{2,1,0:T(8,128)S(1)} %multiply_add_fusion.6), channel_id=1, source_target_pairs={{0,16},{16,32},{32,48},{48,64},{64,80},{80,96},{96,112},{112,128},... | collective-permute-start | bytes 663560 | tf_op jit(solution)/shard_map/while/body/eval_jaxpr/ppermute | solution.py:19
  210.1 7.5 %collective-permute-start.1 = (f32[36,12,128]{2,1,0:T(8,128)S(1)}, f32[36,12,128]{2,1,0:T(8,128)S(1)}, u32[]{:S(2)}, u32[]{:S(2)}) collective-permute-start(f32[36,12,128]{2,1,0:T(8,128)S(1)} %multiply_add_fusion.7), channel_id=1, source_target_pairs={{16,0},{32,16},{48,32},{64,48},{80,64},{96,80},{112,96},{128,112},... | collective-permute-start | bytes 663560 | tf_op jit(solution)/shard_map/while/body/eval_jaxpr/ppermute | solution.py:19
  217.6 8.0 %collective-permute-start = (f32[36,12,128]{2,1,0:T(8,128)S(1)}, f32[36,12,128]{2,1,0:T(8,128)S(1)}, u32[]{:S(2)}, u32[]{:S(2)}) collective-permute-start(f32[36,12,128]{2,1,0:T(8,128)S(1)} %multiply_add_fusion.6), channel_id=1, source_target_pairs={{0,16},{16,32},{32,48},{48,64},{64,80},{80,96},{96,112},{112,128},... | collective-permute-start | bytes 663560 | tf_op jit(solution)/shard_map/while/body/eval_jaxpr/ppermute | solution.py:19
  222.0 7.5 %collective-permute-start.1 = (f32[36,12,128]{2,1,0:T(8,128)S(1)}, f32[36,12,128]{2,1,0:T(8,128)S(1)}, u32[]{:S(2)}, u32[]{:S(2)}) collective-permute-start(f32[36,12,128]{2,1,0:T(8,128)S(1)} %multiply_add_fusion.7), channel_id=1, source_target_pairs={{16,0},{32,16},{48,32},{64,48},{80,64},{96,80},{112,96},{128,112},... | collective-permute-start | bytes 663560 | tf_op jit(solution)/shard_map/while/body/eval_jaxpr/ppermute | solution.py:19
  229.5 1.0 copy-start.1
  229.5 1.1 copy-start.2
  232.6 45.0 %copy-start.3 = (f32[25,256]{1,0:T(8,128)S(1)}, f32[25,256]{1,0:T(8,128)}, u32[]{:S(2)}) copy-start(f32[25,256]{1,0:T(8,128)} %param.15) | copy-start | bytes 76804
  277.6 5.1 copy-start.4
  277.6 5.1 copy-start.5
  277.7 5.1 collective-permute-start.2
  281.4 4.6 collective-permute-start.3
  286.1 5.1 collective-permute-start.4
  289.9 4.3 collective-permute-start.5
  294.3 5.3 %collective-permute-start.6 = (f32[5,1,128]{2,1,0:T(1,128)S(1)}, f32[5,1,128]{2,1,0:T(1,128)S(1)}, u32[]{:S(2)}, u32[]{:S(2)}) collective-permute-start(f32[5,1,128]{2,1,0:T(1,128)S(1)} %get-tuple-element.91), channel_id=1, source_target_pairs={{0,16},{16,32},{32,48},{48,64},{64,80},{80,96},{96,112},{112,128},... | collective-permute-start | bytes 7688 | tf_op jit(solution)/shard_map/ppermute | solution.py:29
  298.4 4.3 collective-permute-start.7
  302.8 5.3 %collective-permute-start.8 = (f32[5,1,128]{2,1,0:T(1,128)S(1)}, f32[5,1,128]{2,1,0:T(1,128)S(1)}, u32[]{:S(2)}, u32[]{:S(2)}) collective-permute-start(f32[5,1,128]{2,1,0:T(1,128)S(1)} %get-tuple-element.87), channel_id=1, source_target_pairs={{0,16},{16,32},{32,48},{48,64},{64,80},{80,96},{96,112},{112,128},... | collective-permute-start | bytes 7688 | tf_op jit(solution)/shard_map/ppermute | solution.py:29
  306.9 4.3 collective-permute-start.9
where the time goes:
time: 532 us; the launch traced here: 530 us
  blocking collectives  260 us (49%)
  waiting for transfers between devices  116 us (22%)
  starting transfers between devices  100 us (19%)
  between operations  16.2 us (3%)
  local copies, waits for them, and re-layouts  15.9 us (3%)
  other arithmetic  14.6 us (3%)
  matrix products  6.31 us (1%)
    psum x2, blocking collectives, body(): lax.psum(newton_sums(loaded, signed, shift_mass, shift_flow), ('sec', 've...  157 us
    ppermute x30, waiting for transfers between devices, passed_along(): return lax.ppermute(block, axis, route)  104 us
    ppermute x30, starting transfers between devices, passed_along(): return lax.ppermute(block, axis, route)  79.3 us
    psum x1, blocking collectives, body(): lax.psum(jnp.dot(weighted, half_field, precision=HIGH), 'vel')  44.9 us
    psum x1, blocking collectives, body(): goals = lax.psum(local_totals, 'sec')  30.6 us
    psum x1, blocking collectives, body(): lax.psum(jnp.dot(weighted, distribution, precision=HIGH), 'vel')  27.9 us
    ppermute x4, starting transfers between devices, extended(): before = lax.ppermute(last, axis, up)  15.5 us
    ppermute x4, waiting for transfers between devices, extended(): after = lax.ppermute(first, axis, down)  12.3 us
  transfers between devices with their start and end apart: 38, of which 34 were waited for; matrix products, arithmetic and copies ran while one was open for 0% of the time, Pallas kernels for 0%

commit v1 on v0

--- a/solution.py
+++ b/solution.py
@@ -1,3 +1,4 @@
+import functools
 import math
 import jax
 import jax.numpy as jnp
@@ -11,6 +12,14 @@
 NEWTON = 2
 HIGH = lax.Precision.HIGHEST
 pseudo_rate = 1.0
+
+
+def open_the_sites(xx, peer_axis, chip_axis):
+    reached = lax.psum(xx, axis_name=peer_axis)
+    return lax.psum(reached, axis_name=chip_axis)
+
+
+lead_quotas_by_axis = functools.partial(open_the_sites, peer_axis="sec", chip_axis="vel")
 
 
 def passed_along(block, axis, distance):
@@ -191,7 +200,7 @@
     goals = lax.psum(local_totals, "sec")
     loaded = node_mass * magnitude
     for newton_turn in range(NEWTON):
-        sums = lax.psum(newton_sums(loaded, signed, shift_mass, shift_flow), ("sec", "vel"))
+        sums = lead_quotas_by_axis(newton_sums(loaded, signed, shift_mass, shift_flow))
         shift_mass, shift_flow = newton_update(shift_mass, shift_flow, sums, goals[0], goals[1])
     growth = jnp.exp(shift_mass + shift_flow * signed)
     new_distribution = synthetic + jnp.abs(synthetic) * (growth[:, None] - 1.0)

time: 532 us -> 469 us (0.88)
  blocking collectives: 260 us -> 197 us
    psum x3 -> x4, blocking collectives: 188 us -> 124 us  [the longest x2 65.4 us: open_the_sites(): return lax.psum(reached, axis_name=chip_axis)]
where the time goes in v1:
time: 469 us; the launch traced here: 467 us
  blocking collectives  197 us (42%)
  waiting for transfers between devices  116 us (25%)
  starting transfers between devices  100 us (21%)
  between operations  16.2 us (3%)
  local copies, waits for them, and re-layouts  16 us (3%)
  other arithmetic  14.6 us (3%)
  matrix products  6.31 us (1%)
    ppermute x30, waiting for transfers between devices, passed_along(): return lax.ppermute(block, axis, route)  104 us
    ppermute x30, starting transfers between devices, passed_along(): return lax.ppermute(block, axis, route)  79.3 us
    psum x2, blocking collectives, open_the_sites(): return lax.psum(reached, axis_name=chip_axis)  65.4 us
    psum x2, blocking collectives, open_the_sites(): reached = lax.psum(xx, axis_name=peer_axis)  59.1 us
    psum x1, blocking collectives, body(): lax.psum(jnp.dot(weighted, half_field, precision=HIGH), 'vel')  44.9 us
    psum x1, blocking collectives, body(): lax.psum(jnp.dot(weighted, distribution, precision=HIGH), 'vel')  27.9 us
    ppermute x4, starting transfers between devices, extended(): before = lax.ppermute(last, axis, up)  15.5 us
    ppermute x4, waiting for transfers between devices, extended(): after = lax.ppermute(first, axis, down)  12.3 us
  transfers between devices with their start and end apart: 38, of which 34 were waited for; matrix products, arithmetic and copies ran while one was open for 0% of the time, Pallas kernels for 0%

profile of v1, /device:TPU:1, one launch (start us, length us, event | category | flops | bytes accessed | tf_op | source)
XLA Modules:
  0.0 466.8 jit_solution(12689609594375236476)
XLA Ops:
  3.6 27.9 %psum.49 = f32[5,256]{1,0:T(8,128)S(1)} all-reduce(f32[5,256]{1,0:T(8,128)S(1)} %fusion.12), channel_id=1, replica_groups=mesh['sec'=16,'vel'=16] {'vel'}, use_global_device_ids=true, to_apply=%region_0.0 | all-reduce | flops 1280 | bytes 10240 | tf_op jit(solution)/shard_map/psum | solution.py:148
  39.4 2.0 rev.8
  41.5 2.0 rev.9
  44.4 185.1 %while.12 = (s32[]{:T(128)}, f32[36,12,128]{2,1,0:T(8,128)S(1)}, f32[36,12,128]{2,1,0:T(8,128)S(1)}, f32[36,12,128]{2,1,0:T(8,128)S(1)}, f32[36,12,128]{2,1,0:T(...) while((s32[]{:T(128)}, f32[36,12,128]{2,1,0:T(8,128)S(1)}, ...), condition=%wide.region_2.0_spmd, body=%wide.region_1.0_spmd.sunk | while | flops 221186 | bytes 3539109 | solution.py:177
  44.5 3.2 collective-permute-start
  49.1 2.3 collective-permute-done
  51.3 3.9 collective-permute-done.1
  55.3 3.5 collective-permute-start
  60.2 2.3 collective-permute-done
  62.4 3.9 collective-permute-done.1
  66.4 4.4 collective-permute-start
  72.2 2.3 collective-permute-done
  74.5 3.9 collective-permute-done.1
  78.4 4.0 collective-permute-start
  83.9 2.3 collective-permute-done
  86.1 3.9 collective-permute-done.1
  90.1 4.0 collective-permute-start
  95.5 2.3 collective-permute-done
  97.7 3.9 collective-permute-done.1
  101.7 3.7 collective-permute-start
  106.8 2.3 collective-permute-done
  109.1 4.0 collective-permute-done.1
  113.1 3.9 collective-permute-start
  118.5 3.2 collective-permute-done
  121.7 4.2 collective-permute-done.1
  125.9 3.7 collective-permute-start
  131.0 4.3 collective-permute-done
  135.3 4.4 collective-permute-done.1
  139.8 3.7 collective-permute-start
  144.9 5.2 %collective-permute-done = f32[36,12,128]{2,1,0:T(8,128)S(1)} collective-permute-done((f32[36,12,128]{2,1,0:T(8,128)S(1)}, f32[36,12,128]{2,1,0:T(8,128)S(1)}, u32[]{:S(2)}, u32[]{:S(2)}) %collective-permute-start) | collective-permute-done | bytes 221216 | tf_op jit(solution)/shard_map/while/body/eval_jaxpr/ppermute | solution.py:28
  150.1 4.2 collective-permute-done.1
  154.3 3.8 collective-permute-start
  159.6 4.3 collective-permute-done
  163.9 3.9 collective-permute-done.1
  167.8 4.8 %collective-permute-start = (f32[36,12,128]{2,1,0:T(8,128)S(1)}, f32[36,12,128]{2,1,0:T(8,128)S(1)}, u32[]{:S(2)}, u32[]{:S(2)}) collective-permute-start(f32[36,12,128]{2,1,0:T(8,128)S(1)} %multiply_add_fusion.6), channel_id=1, source_target_pairs={{0,16},{16,32},{32,48},{48,64},{64,80},{80,96},{96,112},{112,128},... | collective-permute-start | bytes 663560 | tf_op jit(solution)/shard_map/while/body/eval_jaxpr/ppermute | solution.py:28
  174.0 3.7 collective-permute-done
  177.7 3.9 collective-permute-done.1
  181.7 4.3 collective-permute-start
  187.3 2.7 collective-permute-done
  190.1 3.9 collective-permute-done.1
  194.1 4.3 collective-permute-start
  199.7 2.3 collective-permute-done
  202.0 3.9 collective-permute-done.1
  206.0 4.0 collective-permute-start
  211.4 2.3 collective-permute-done
  213.6 3.9 collective-permute-done.1
  217.6 4.3 collective-permute-start
  223.3 2.3 collective-permute-done
  225.6 3.9 collective-permute-done.1
  232.6 44.9 %psum.50 = f32[5,256]{1,0:T(8,128)S(1)} all-reduce(f32[5,256]{1,0:T(8,128)S(1)} %fusion), channel_id=1, replica_groups=mesh['sec'=16,'vel'=16] {'vel'}, use_global_device_ids=true, to_apply=%region_3.0 | all-reduce | flops 1280 | bytes 10240 | tf_op jit(solution)/shard_map/psum | solution.py:181
  277.7 3.7 collective-permute-start.2
  282.8 3.2 collective-permute-done.3
  286.1 3.7 collective-permute-start.4
  291.2 3.0 collective-permute-done.5
  294.3 4.0 collective-permute-start.6
  299.7 3.0 collective-permute-done.7
  302.8 4.0 collective-permute-start.8
  308.2 3.0 collective-permute-done.9
  315.5 3.2 stack.41
  318.7 30.6 %all-reduce.8 = (f32[5]{0:T(128)S(1)}, f32[2]{0:T(128)S(1)}) all-reduce(f32[5]{0:T(128)S(1)} %stack.41, f32[2]{0:T(128)S(1)} %bitcast.57), channel_id=1, replica_groups=mesh['sec'=16,'vel'=16] {'sec'}, use_global_device_ids=true, to_apply=%region_23.0 | all-reduce | flops 7 | bytes 56 | tf_op jit(solution)/shard_map/psum | solution.py:18
  349.3 34.9 %psum.52 = f32[5]{0:T(128)S(1)} all-reduce(f32[5]{0:T(128)S(1)} %get-tuple-element.73), channel_id=1, replica_groups=mesh['sec'=16,'vel'=16] {'vel'}, use_global_device_ids=true, to_apply=%region_24.0 | all-reduce | flops 5 | bytes 40 | tf_op jit(solution)/shard_map/psum | solution.py:19
  394.6 3.2 stack.47
  397.8 28.5 %psum.54 = f32[5]{0:T(128)S(1)} all-reduce(f32[5]{0:T(128)S(1)} %stack.47), channel_id=1, replica_groups=mesh['sec'=16,'vel'=16] {'sec'}, use_global_device_ids=true, to_apply=%region_32.0 | all-reduce | flops 5 | bytes 40 | tf_op jit(solution)/shard_map/psum | solution.py:18
  426.2 30.5 %psum.55 = f32[5]{0:T(128)S(1)} all-reduce(f32[5]{0:T(128)S(1)} %psum.54), channel_id=1, replica_groups=mesh['sec'=16,'vel'=16] {'vel'}, use_global_device_ids=true, to_apply=%region_33.0 | all-reduce | flops 5 | bytes 40 | tf_op jit(solution)/shard_map/psum | solution.py:19
  (127 shorter events, 51.0 us)
Async XLA Ops:
  0.6 1.7 copy-start
  34.7 0.7 copy-start.6
  44.5 6.9 %collective-permute-start = (f32[36,12,128]{2,1,0:T(8,128)S(1)}, f32[36,12,128]{2,1,0:T(8,128)S(1)}, u32[]{:S(2)}, u32[]{:S(2)}) collective-permute-start(f32[36,12,128]{2,1,0:T(8,128)S(1)} %multiply_add_fusion.6), channel_id=1, source_target_pairs={{0,16},{16,32},{32,48},{48,64},{64,80},{80,96},{96,112},{112,128},... | collective-permute-start | bytes 663560 | tf_op jit(solution)/shard_map/while/body/eval_jaxpr/ppermute | solution.py:28
  47.8 7.5 %collective-permute-start.1 = (f32[36,12,128]{2,1,0:T(8,128)S(1)}, f32[36,12,128]{2,1,0:T(8,128)S(1)}, u32[]{:S(2)}, u32[]{:S(2)}) collective-permute-start(f32[36,12,128]{2,1,0:T(8,128)S(1)} %multiply_add_fusion.7), channel_id=1, source_target_pairs={{16,0},{32,16},{48,32},{64,48},{80,64},{96,80},{112,96},{128,112},... | collective-permute-start | bytes 663560 | tf_op jit(solution)/shard_map/while/body/eval_jaxpr/ppermute | solution.py:28
  55.3 7.1 %collective-permute-start = (f32[36,12,128]{2,1,0:T(8,128)S(1)}, f32[36,12,128]{2,1,0:T(8,128)S(1)}, u32[]{:S(2)}, u32[]{:S(2)}) collective-permute-start(f32[36,12,128]{2,1,0:T(8,128)S(1)} %multiply_add_fusion.6), channel_id=1, source_target_pairs={{0,16},{16,32},{32,48},{48,64},{64,80},{80,96},{96,112},{112,128},... | collective-permute-start | bytes 663560 | tf_op jit(solution)/shard_map/while/body/eval_jaxpr/ppermute | solution.py:28
  58.9 7.5 %collective-permute-start.1 = (f32[36,12,128]{2,1,0:T(8,128)S(1)}, f32[36,12,128]{2,1,0:T(8,128)S(1)}, u32[]{:S(2)}, u32[]{:S(2)}) collective-permute-start(f32[36,12,128]{2,1,0:T(8,128)S(1)} %multiply_add_fusion.7), channel_id=1, source_target_pairs={{16,0},{32,16},{48,32},{64,48},{80,64},{96,80},{112,96},{128,112},... | collective-permute-start | bytes 663560 | tf_op jit(solution)/shard_map/while/body/eval_jaxpr/ppermute | solution.py:28
  66.4 8.1 %collective-permute-start = (f32[36,12,128]{2,1,0:T(8,128)S(1)}, f32[36,12,128]{2,1,0:T(8,128)S(1)}, u32[]{:S(2)}, u32[]{:S(2)}) collective-permute-start(f32[36,12,128]{2,1,0:T(8,128)S(1)} %multiply_add_fusion.6), channel_id=1, source_target_pairs={{0,16},{16,32},{32,48},{48,64},{64,80},{80,96},{96,112},{112,128},... | collective-permute-start | bytes 663560 | tf_op jit(solution)/shard_map/while/body/eval_jaxpr/ppermute | solution.py:28
  70.9 7.5 %collective-permute-start.1 = (f32[36,12,128]{2,1,0:T(8,128)S(1)}, f32[36,12,128]{2,1,0:T(8,128)S(1)}, u32[]{:S(2)}, u32[]{:S(2)}) collective-permute-start(f32[36,12,128]{2,1,0:T(8,128)S(1)} %multiply_add_fusion.7), channel_id=1, source_target_pairs={{16,0},{32,16},{48,32},{64,48},{80,64},{96,80},{112,96},{128,112},... | collective-permute-start | bytes 663560 | tf_op jit(solution)/shard_map/while/body/eval_jaxpr/ppermute | solution.py:28
  78.4 7.7 %collective-permute-start = (f32[36,12,128]{2,1,0:T(8,128)S(1)}, f32[36,12,128]{2,1,0:T(8,128)S(1)}, u32[]{:S(2)}, u32[]{:S(2)}) collective-permute-start(f32[36,12,128]{2,1,0:T(8,128)S(1)} %multiply_add_fusion.6), channel_id=1, source_target_pairs={{0,16},{16,32},{32,48},{48,64},{64,80},{80,96},{96,112},{112,128},... | collective-permute-start | bytes 663560 | tf_op jit(solution)/shard_map/while/body/eval_jaxpr/ppermute | solution.py:28
  82.5 7.5 %collective-permute-start.1 = (f32[36,12,128]{2,1,0:T(8,128)S(1)}, f32[36,12,128]{2,1,0:T(8,128)S(1)}, u32[]{:S(2)}, u32[]{:S(2)}) collective-permute-start(f32[36,12,128]{2,1,0:T(8,128)S(1)} %multiply_add_fusion.7), channel_id=1, source_target_pairs={{16,0},{32,16},{48,32},{64,48},{80,64},{96,80},{112,96},{128,112},... | collective-permute-start | bytes 663560 | tf_op jit(solution)/shard_map/while/body/eval_jaxpr/ppermute | solution.py:28
  90.1 7.7 %collective-permute-start = (f32[36,12,128]{2,1,0:T(8,128)S(1)}, f32[36,12,128]{2,1,0:T(8,128)S(1)}, u32[]{:S(2)}, u32[]{:S(2)}) collective-permute-start(f32[36,12,128]{2,1,0:T(8,128)S(1)} %multiply_add_fusion.6), channel_id=1, source_target_pairs={{0,16},{16,32},{32,48},{48,64},{64,80},{80,96},{96,112},{112,128},... | collective-permute-start | bytes 663560 | tf_op jit(solution)/shard_map/while/body/eval_jaxpr/ppermute | solution.py:28
  94.2 7.5 %collective-permute-start.1 = (f32[36,12,128]{2,1,0:T(8,128)S(1)}, f32[36,12,128]{2,1,0:T(8,128)S(1)}, u32[]{:S(2)}, u32[]{:S(2)}) collective-permute-start(f32[36,12,128]{2,1,0:T(8,128)S(1)} %multiply_add_fusion.7), channel_id=1, source_target_pairs={{16,0},{32,16},{48,32},{64,48},{80,64},{96,80},{112,96},{128,112},... | collective-permute-start | bytes 663560 | tf_op jit(solution)/shard_map/while/body/eval_jaxpr/ppermute | solution.py:28
  101.7 7.4 %collective-permute-start = (f32[36,12,128]{2,1,0:T(8,128)S(1)}, f32[36,12,128]{2,1,0:T(8,128)S(1)}, u32[]{:S(2)}, u32[]{:S(2)}) collective-permute-start(f32[36,12,128]{2,1,0:T(8,128)S(1)} %multiply_add_fusion.6), channel_id=1, source_target_pairs={{0,16},{16,32},{32,48},{48,64},{64,80},{80,96},{96,112},{112,128},... | collective-permute-start | bytes 663560 | tf_op jit(solution)/shard_map/while/body/eval_jaxpr/ppermute | solution.py:28
  105.5 7.6 %collective-permute-start.1 = (f32[36,12,128]{2,1,0:T(8,128)S(1)}, f32[36,12,128]{2,1,0:T(8,128)S(1)}, u32[]{:S(2)}, u32[]{:S(2)}) collective-permute-start(f32[36,12,128]{2,1,0:T(8,128)S(1)} %multiply_add_fusion.7), channel_id=1, source_target_pairs={{16,0},{32,16},{48,32},{64,48},{80,64},{96,80},{112,96},{128,112},... | collective-permute-start | bytes 663560 | tf_op jit(solution)/shard_map/while/body/eval_jaxpr/ppermute | solution.py:28
  113.1 8.5 %collective-permute-start = (f32[36,12,128]{2,1,0:T(8,128)S(1)}, f32[36,12,128]{2,1,0:T(8,128)S(1)}, u32[]{:S(2)}, u32[]{:S(2)}) collective-permute-start(f32[36,12,128]{2,1,0:T(8,128)S(1)} %multiply_add_fusion.6), channel_id=1, source_target_pairs={{0,16},{16,32},{32,48},{48,64},{64,80},{80,96},{96,112},{112,128},... | collective-permute-start | bytes 663560 | tf_op jit(solution)/shard_map/while/body/eval_jaxpr/ppermute | solution.py:28
  117.2 8.7 %collective-permute-start.1 = (f32[36,12,128]{2,1,0:T(8,128)S(1)}, f32[36,12,128]{2,1,0:T(8,128)S(1)}, u32[]{:S(2)}, u32[]{:S(2)}) collective-permute-start(f32[36,12,128]{2,1,0:T(8,128)S(1)} %multiply_add_fusion.7), channel_id=1, source_target_pairs={{16,0},{32,16},{48,32},{64,48},{80,64},{96,80},{112,96},{128,112},... | collective-permute-start | bytes 663560 | tf_op jit(solution)/shard_map/while/body/eval_jaxpr/ppermute | solution.py:28
  125.9 9.4 %collective-permute-start = (f32[36,12,128]{2,1,0:T(8,128)S(1)}, f32[36,12,128]{2,1,0:T(8,128)S(1)}, u32[]{:S(2)}, u32[]{:S(2)}) collective-permute-start(f32[36,12,128]{2,1,0:T(8,128)S(1)} %multiply_add_fusion.6), channel_id=1, source_target_pairs={{0,16},{16,32},{32,48},{48,64},{64,80},{80,96},{96,112},{112,128},... | collective-permute-start | bytes 663560 | tf_op jit(solution)/shard_map/while/body/eval_jaxpr/ppermute | solution.py:28
  129.7 10.1 %collective-permute-start.1 = (f32[36,12,128]{2,1,0:T(8,128)S(1)}, f32[36,12,128]{2,1,0:T(8,128)S(1)}, u32[]{:S(2)}, u32[]{:S(2)}) collective-permute-start(f32[36,12,128]{2,1,0:T(8,128)S(1)} %multiply_add_fusion.7), channel_id=1, source_target_pairs={{16,0},{32,16},{48,32},{64,48},{80,64},{96,80},{112,96},{128,112},... | collective-permute-start | bytes 663560 | tf_op jit(solution)/shard_map/while/body/eval_jaxpr/ppermute | solution.py:28
  139.8 10.2 %collective-permute-start = (f32[36,12,128]{2,1,0:T(8,128)S(1)}, f32[36,12,128]{2,1,0:T(8,128)S(1)}, u32[]{:S(2)}, u32[]{:S(2)}) collective-permute-start(f32[36,12,128]{2,1,0:T(8,128)S(1)} %multiply_add_fusion.6), channel_id=1, source_target_pairs={{0,16},{16,32},{32,48},{48,64},{64,80},{80,96},{96,112},{112,128},... | collective-permute-start | bytes 663560 | tf_op jit(solution)/shard_map/while/body/eval_jaxpr/ppermute | solution.py:28
  143.6 10.7 %collective-permute-start.1 = (f32[36,12,128]{2,1,0:T(8,128)S(1)}, f32[36,12,128]{2,1,0:T(8,128)S(1)}, u32[]{:S(2)}, u32[]{:S(2)}) collective-permute-start(f32[36,12,128]{2,1,0:T(8,128)S(1)} %multiply_add_fusion.7), channel_id=1, source_target_pairs={{16,0},{32,16},{48,32},{64,48},{80,64},{96,80},{112,96},{128,112},... | collective-permute-start | bytes 663560 | tf_op jit(solution)/shard_map/while/body/eval_jaxpr/ppermute | solution.py:28
  154.3 9.5 %collective-permute-start = (f32[36,12,128]{2,1,0:T(8,128)S(1)}, f32[36,12,128]{2,1,0:T(8,128)S(1)}, u32[]{:S(2)}, u32[]{:S(2)}) collective-permute-start(f32[36,12,128]{2,1,0:T(8,128)S(1)} %multiply_add_fusion.6), channel_id=1, source_target_pairs={{0,16},{16,32},{32,48},{48,64},{64,80},{80,96},{96,112},{112,128},... | collective-permute-start | bytes 663560 | tf_op jit(solution)/shard_map/while/body/eval_jaxpr/ppermute | solution.py:28
  158.3 9.5 %collective-permute-start.1 = (f32[36,12,128]{2,1,0:T(8,128)S(1)}, f32[36,12,128]{2,1,0:T(8,128)S(1)}, u32[]{:S(2)}, u32[]{:S(2)}) collective-permute-start(f32[36,12,128]{2,1,0:T(8,128)S(1)} %multiply_add_fusion.7), channel_id=1, source_target_pairs={{16,0},{32,16},{48,32},{64,48},{80,64},{96,80},{112,96},{128,112},... | collective-permute-start | bytes 663560 | tf_op jit(solution)/shard_map/while/body/eval_jaxpr/ppermute | solution.py:28
  167.8 9.9 %collective-permute-start = (f32[36,12,128]{2,1,0:T(8,128)S(1)}, f32[36,12,128]{2,1,0:T(8,128)S(1)}, u32[]{:S(2)}, u32[]{:S(2)}) collective-permute-start(f32[36,12,128]{2,1,0:T(8,128)S(1)} %multiply_add_fusion.6), channel_id=1, source_target_pairs={{0,16},{16,32},{32,48},{48,64},{64,80},{80,96},{96,112},{112,128},... | collective-permute-start | bytes 663560 | tf_op jit(solution)/shard_map/while/body/eval_jaxpr/ppermute | solution.py:28
  172.7 8.9 %collective-permute-start.1 = (f32[36,12,128]{2,1,0:T(8,128)S(1)}, f32[36,12,128]{2,1,0:T(8,128)S(1)}, u32[]{:S(2)}, u32[]{:S(2)}) collective-permute-start(f32[36,12,128]{2,1,0:T(8,128)S(1)} %multiply_add_fusion.7), channel_id=1, source_target_pairs={{16,0},{32,16},{48,32},{64,48},{80,64},{96,80},{112,96},{128,112},... | collective-permute-start | bytes 663560 | tf_op jit(solution)/shard_map/while/body/eval_jaxpr/ppermute | solution.py:28
  181.7 8.4 %collective-permute-start = (f32[36,12,128]{2,1,0:T(8,128)S(1)}, f32[36,12,128]{2,1,0:T(8,128)S(1)}, u32[]{:S(2)}, u32[]{:S(2)}) collective-permute-start(f32[36,12,128]{2,1,0:T(8,128)S(1)} %multiply_add_fusion.6), channel_id=1, source_target_pairs={{0,16},{16,32},{32,48},{48,64},{64,80},{80,96},{96,112},{112,128},... | collective-permute-start | bytes 663560 | tf_op jit(solution)/shard_map/while/body/eval_jaxpr/ppermute | solution.py:28
  186.0 8.0 %collective-permute-start.1 = (f32[36,12,128]{2,1,0:T(8,128)S(1)}, f32[36,12,128]{2,1,0:T(8,128)S(1)}, u32[]{:S(2)}, u32[]{:S(2)}) collective-permute-start(f32[36,12,128]{2,1,0:T(8,128)S(1)} %multiply_add_fusion.7), channel_id=1, source_target_pairs={{16,0},{32,16},{48,32},{64,48},{80,64},{96,80},{112,96},{128,112},... | collective-permute-start | bytes 663560 | tf_op jit(solution)/shard_map/while/body/eval_jaxpr/ppermute | solution.py:28
  194.1 8.0 %collective-permute-start = (f32[36,12,128]{2,1,0:T(8,128)S(1)}, f32[36,12,128]{2,1,0:T(8,128)S(1)}, u32[]{:S(2)}, u32[]{:S(2)}) collective-permute-start(f32[36,12,128]{2,1,0:T(8,128)S(1)} %multiply_add_fusion.6), channel_id=1, source_target_pairs={{0,16},{16,32},{32,48},{48,64},{64,80},{80,96},{96,112},{112,128},... | collective-permute-start | bytes 663560 | tf_op jit(solution)/shard_map/while/body/eval_jaxpr/ppermute | solution.py:28
  198.4 7.5 %collective-permute-start.1 = (f32[36,12,128]{2,1,0:T(8,128)S(1)}, f32[36,12,128]{2,1,0:T(8,128)S(1)}, u32[]{:S(2)}, u32[]{:S(2)}) collective-permute-start(f32[36,12,128]{2,1,0:T(8,128)S(1)} %multiply_add_fusion.7), channel_id=1, source_target_pairs={{16,0},{32,16},{48,32},{64,48},{80,64},{96,80},{112,96},{128,112},... | collective-permute-start | bytes 663560 | tf_op jit(solution)/shard_map/while/body/eval_jaxpr/ppermute | solution.py:28
  206.0 7.7 %collective-permute-start = (f32[36,12,128]{2,1,0:T(8,128)S(1)}, f32[36,12,128]{2,1,0:T(8,128)S(1)}, u32[]{:S(2)}, u32[]{:S(2)}) collective-permute-start(f32[36,12,128]{2,1,0:T(8,128)S(1)} %multiply_add_fusion.6), channel_id=1, source_target_pairs={{0,16},{16,32},{32,48},{48,64},{64,80},{80,96},{96,112},{112,128},... | collective-permute-start | bytes 663560 | tf_op jit(solution)/shard_map/while/body/eval_jaxpr/ppermute | solution.py:28
  210.1 7.5 %collective-permute-start.1 = (f32[36,12,128]{2,1,0:T(8,128)S(1)}, f32[36,12,128]{2,1,0:T(8,128)S(1)}, u32[]{:S(2)}, u32[]{:S(2)}) collective-permute-start(f32[36,12,128]{2,1,0:T(8,128)S(1)} %multiply_add_fusion.7), channel_id=1, source_target_pairs={{16,0},{32,16},{48,32},{64,48},{80,64},{96,80},{112,96},{128,112},... | collective-permute-start | bytes 663560 | tf_op jit(solution)/shard_map/while/body/eval_jaxpr/ppermute | solution.py:28
  217.6 8.0 %collective-permute-start = (f32[36,12,128]{2,1,0:T(8,128)S(1)}, f32[36,12,128]{2,1,0:T(8,128)S(1)}, u32[]{:S(2)}, u32[]{:S(2)}) collective-permute-start(f32[36,12,128]{2,1,0:T(8,128)S(1)} %multiply_add_fusion.6), channel_id=1, source_target_pairs={{0,16},{16,32},{32,48},{48,64},{64,80},{80,96},{96,112},{112,128},... | collective-permute-start | bytes 663560 | tf_op jit(solution)/shard_map/while/body/eval_jaxpr/ppermute | solution.py:28
  222.0 7.5 %collective-permute-start.1 = (f32[36,12,128]{2,1,0:T(8,128)S(1)}, f32[36,12,128]{2,1,0:T(8,128)S(1)}, u32[]{:S(2)}, u32[]{:S(2)}) collective-permute-start(f32[36,12,128]{2,1,0:T(8,128)S(1)} %multiply_add_fusion.7), channel_id=1, source_target_pairs={{16,0},{32,16},{48,32},{64,48},{80,64},{96,80},{112,96},{128,112},... | collective-permute-start | bytes 663560 | tf_op jit(solution)/shard_map/while/body/eval_jaxpr/ppermute | solution.py:28
  229.5 1.0 copy-start.1
  229.5 1.1 copy-start.2
  232.6 45.0 %copy-start.3 = (f32[25,256]{1,0:T(8,128)S(1)}, f32[25,256]{1,0:T(8,128)}, u32[]{:S(2)}) copy-start(f32[25,256]{1,0:T(8,128)} %param.15) | copy-start | bytes 76804
  277.6 5.1 %copy-start.4 = (f32[25,256]{1,0:T(8,128)S(1)}, f32[25,256]{1,0:T(8,128)}, u32[]{:S(2)}) copy-start(f32[25,256]{1,0:T(8,128)} %param.13) | copy-start | bytes 76804
  277.6 5.1 %copy-start.5 = (f32[25,256]{1,0:T(8,128)S(1)}, f32[25,256]{1,0:T(8,128)}, u32[]{:S(2)}) copy-start(f32[25,256]{1,0:T(8,128)} %param.14) | copy-start | bytes 76804
  277.7 5.1 %collective-permute-start.2 = (f32[5,1,128]{2,1,0:T(1,128)S(1)}, f32[5,1,128]{2,1,0:T(1,128)S(1)}, u32[]{:S(2)}, u32[]{:S(2)}) collective-permute-start(f32[5,1,128]{2,1,0:T(1,128)S(1)} %get-tuple-element.101), channel_id=1, source_target_pairs={{0,16},{16,32},{32,48},{48,64},{64,80},{80,96},{96,112},{112,128},... | collective-permute-start | bytes 7688 | tf_op jit(solution)/shard_map/ppermute | solution.py:38
  281.4 4.6 collective-permute-start.3
  286.1 5.1 %collective-permute-start.4 = (f32[5,1,128]{2,1,0:T(1,128)S(1)}, f32[5,1,128]{2,1,0:T(1,128)S(1)}, u32[]{:S(2)}, u32[]{:S(2)}) collective-permute-start(f32[5,1,128]{2,1,0:T(1,128)S(1)} %get-tuple-element.97), channel_id=1, source_target_pairs={{0,16},{16,32},{32,48},{48,64},{64,80},{80,96},{96,112},{112,128},... | collective-permute-start | bytes 7688 | tf_op jit(solution)/shard_map/ppermute | solution.py:38
  289.9 4.3 collective-permute-start.5
  294.3 5.3 %collective-permute-start.6 = (f32[5,1,128]{2,1,0:T(1,128)S(1)}, f32[5,1,128]{2,1,0:T(1,128)S(1)}, u32[]{:S(2)}, u32[]{:S(2)}) collective-permute-start(f32[5,1,128]{2,1,0:T(1,128)S(1)} %get-tuple-element.93), channel_id=1, source_target_pairs={{0,16},{16,32},{32,48},{48,64},{64,80},{80,96},{96,112},{112,128},... | collective-permute-start | bytes 7688 | tf_op jit(solution)/shard_map/ppermute | solution.py:38
  298.4 4.3 collective-permute-start.7
  302.8 5.3 %collective-permute-start.8 = (f32[5,1,128]{2,1,0:T(1,128)S(1)}, f32[5,1,128]{2,1,0:T(1,128)S(1)}, u32[]{:S(2)}, u32[]{:S(2)}) collective-permute-start(f32[5,1,128]{2,1,0:T(1,128)S(1)} %get-tuple-element.89), channel_id=1, source_target_pairs={{0,16},{16,32},{32,48},{48,64},{64,80},{80,96},{96,112},{112,128},... | collective-permute-start | bytes 7688 | tf_op jit(solution)/shard_map/ppermute | solution.py:38
  306.9 4.3 collective-permute-start.9
